TPU v7x, 512 devices: a whole 4x8x8 slice. The times are simulated.
512 devices in a mesh: req: 64 (over x, y, core), tp: 8 (over z).
Axes of the slice: x: 4, y: 8, z: 8, core: 2. Of those that a mesh axis runs over, the one named last changes fastest.
Arguments:
- vit_context: bfloat16 [32768, 4096], P('req', 'tp'), may hold values from -6 to 6
- vision_residual: bfloat16 [32768, 4096], P('req', 'tp'), may hold values from -75 to 75
- out_weight: bfloat16 [4096, 4096], P('tp', 'req'), may hold values from -0.09375 to 0.09375
- layer_scale: float32 [4096], P('tp'), may hold values from 0.2 to 2
- prompt: bfloat16 [64, 256, 4096], P('req', None, 'tp'), may hold values from -75 to 75
- prompt_len: int32 [64], P('req'), may hold values from 128 to 256
- image_at: int32 [64], P('req'), may hold values from 0 to 128
- grid_sizes: int32 [128, 2], replicated, may hold values from 7 to 8, as said below
- image_owner: int32 [128], replicated, may hold values from 0 to 63, as said below
- norm_gain: float32 [4096], replicated, may hold values from 0.5 to 1.5
- qkv_weight: bfloat16 [4096, 6144], P('req', 'tp'), may hold values from -0.09375 to 0.09375
Outputs:
- qkv: bfloat16 [24576, 6144], P('req', 'tp')
Inputs may be any that keep to these rules, and one draw needn't show every extreme that they name: `image_owner`: each request owns exactly 2 images. `grid_sizes`: each side is 7 or 8; in every draw the images of some request are all 8 by 8, so that request has exactly 128 merged rows.
All inputs are finite; a program needn't handle non-finite values.
Results may differ from a plain program's by a relative error of at most 0.008.
Values may be sent and summed in bfloat16 or wider, within the bound.
No kernel may reach another device: no remote copies, remote signals or barrier semaphores. Data moves between devices by JAX's collectives and lax.ppermute only.
A program may use at most 64 MiB of HBM per device.

v0:
```python
import jax
import jax.numpy as jnp
from jax import lax
from jax.sharding import PartitionSpec as P

HEAD = 128
GROUP = 4
IMG_MAX = 128


def request_plan(grid_sizes, image_owner, requests):
    image_rows = grid_sizes[:, 0] * grid_sizes[:, 1]
    member = (image_owner[:, None] == jnp.arange(requests, dtype=jnp.int32)[None, :]).astype(
        jnp.int32
    )
    counts = jnp.sum(image_rows[:, None] * member, axis=0)
    starts = jnp.cumsum(counts) - counts
    return (counts, starts)


def rope_tables(count):
    half_size = HEAD // 2
    exponent = jnp.arange(half_size, dtype=jnp.float32) * (2.0 / HEAD)
    frequency = jnp.exp(-exponent * jnp.log(jnp.float32(500000.0)))
    angles = jnp.arange(count, dtype=jnp.float32)[:, None] * frequency[None, :]
    return (jnp.cos(angles), jnp.sin(angles))


def apply_rope(projected, cosine_table, sine_table):
    seq_rows = projected.shape[0]
    head_blocks = projected.reshape(seq_rows, -1, GROUP + 2, HEAD)
    turning = head_blocks[:, :, : GROUP + 1, :]
    first_half = turning[..., : HEAD // 2]
    second_half = turning[..., HEAD // 2 :]
    cosine_wide = cosine_table[:, None, None, :]
    sine_wide = sine_table[:, None, None, :]
    turned = jnp.concatenate(
        [
            first_half * cosine_wide - second_half * sine_wide,
            second_half * cosine_wide + first_half * sine_wide,
        ],
        axis=-1,
    )
    head_blocks = jnp.concatenate([turned, head_blocks[:, :, GROUP + 1 :, :]], axis=2)
    return head_blocks.reshape(seq_rows, -1)


def normalize(embedded, norm_gain):
    values = embedded.astype(jnp.float32)
    mean_square = jnp.mean(values * values, axis=-1, keepdims=True)
    return (values * lax.rsqrt(mean_square + 1e-05) * norm_gain[None, :]).astype(jnp.bfloat16)


def shards(
    vit_context,
    vision_residual,
    out_weight,
    layer_scale,
    prompt,
    prompt_len,
    image_at,
    grid_sizes,
    image_owner,
    norm_gain,
    qkv_weight,
):
    requests = lax.axis_size("req")
    device_index = lax.axis_index("req")
    feature_width = vit_context.shape[1]
    merged_context = jnp.mean(
        vit_context.astype(jnp.float32).reshape(-1, 4, feature_width), axis=1
    ).astype(jnp.bfloat16)
    merged_residual = jnp.mean(
        vision_residual.astype(jnp.float32).reshape(-1, 4, feature_width), axis=1
    )
    partial_value = jnp.dot(
        merged_context,
        lax.all_gather(out_weight, "req", axis=1, tiled=True),
        preferred_element_type=jnp.float32,
    )
    summed = lax.psum(partial_value.astype(jnp.bfloat16), "tp").astype(jnp.float32)
    own_share = lax.dynamic_slice_in_dim(
        summed, lax.axis_index("tp") * feature_width, feature_width, 1
    )
    merged = (merged_residual + layer_scale[None, :] * own_share).astype(jnp.bfloat16)
    merged_count = merged.shape[0]
    counts, starts = request_plan(grid_sizes, image_owner, requests)
    request_ends = starts + counts
    capacity = (IMG_MAX + requests - 1) // requests
    request_ids = jnp.arange(requests, dtype=jnp.int32)
    group_index = jnp.arange(merged_count, dtype=jnp.int32) * requests + device_index
    destination = jnp.sum((request_ends[None, :] <= group_index[:, None]).astype(jnp.int32), axis=1)
    owned_start = jnp.sum(
        jnp.where(destination[:, None] == request_ids[None, :], starts[None, :], 0), axis=1
    )
    target = destination * capacity + (group_index - owned_start) // requests
    usable = destination < requests
    send_slots = jnp.arange(requests * capacity, dtype=jnp.int32)
    placing = ((send_slots[:, None] == target[None, :]) & usable[None, :]).astype(jnp.bfloat16)
    outgoing = jnp.dot(placing, merged, preferred_element_type=jnp.float32).astype(jnp.bfloat16)
    arrived = lax.all_to_all(
        outgoing.reshape(requests, capacity, feature_width),
        "req",
        split_axis=0,
        concat_axis=0,
        tiled=True,
    )
    arrived = arrived.reshape(requests * capacity, feature_width)
    own_request = request_ids == device_index
    own_count = jnp.sum(jnp.where(own_request, counts, 0))
    own_start = jnp.sum(jnp.where(own_request, starts, 0))
    image_from = image_at[0]
    prompt_count = prompt_len[0]
    seq_slots = prompt.shape[1] + IMG_MAX
    slot_index = jnp.arange(seq_slots, dtype=jnp.int32)
    image_row = slot_index - image_from
    in_image = (image_row >= 0) & (image_row < own_count)
    is_live = slot_index < prompt_count + own_count
    from_prompt = is_live & jnp.logical_not(in_image)
    flat_index = (own_start + image_row) % requests * capacity + image_row // requests
    image_pick = ((flat_index[:, None] == send_slots[None, :]) & in_image[:, None]).astype(
        jnp.bfloat16
    )
    prompt_row = jnp.where(slot_index < image_from, slot_index, slot_index - own_count)
    prompt_ids = jnp.arange(prompt.shape[1], dtype=jnp.int32)
    prompt_pick = ((prompt_row[:, None] == prompt_ids[None, :]) & from_prompt[:, None]).astype(
        jnp.bfloat16
    )
    embedded = (
        jnp.dot(image_pick, arrived, preferred_element_type=jnp.float32)
        + jnp.dot(prompt_pick, prompt[0], preferred_element_type=jnp.float32)
    ).astype(jnp.bfloat16)
    gathered = lax.all_gather(embedded, "tp", axis=1, tiled=True)
    normed = normalize(gathered, norm_gain)
    projected = jnp.dot(
        normed,
        lax.all_gather(qkv_weight, "req", axis=0, tiled=True),
        preferred_element_type=jnp.float32,
    )
    cosine_table, sine_table = rope_tables(seq_slots)
    return apply_rope(projected, cosine_table, sine_table).astype(jnp.bfloat16)


def solution(mesh):
    in_specs = (
        P("req", "tp"),
        P("req", "tp"),
        P("tp", "req"),
        P("tp"),
        P("req", None, "tp"),
        P("req"),
        P("req"),
        P(),
        P(),
        P(),
        P("req", "tp"),
    )
    out_specs = P("req", "tp")
    return jax.shard_map(shards, mesh=mesh, in_specs=in_specs, out_specs=out_specs, check_vma=False)
```

profile of v0, /device:TPU:1, one launch (start us, length us, event | category | flops | bytes accessed | tf_op | source)
XLA Modules:
  0.0 352.9 jit_solution(7770393168710454331)
XLA Ops:
  6.5 0.7 all-gather.4.cloned.1.call-update
  7.3 1.4 reshape.205
  8.7 0.6 reduce_sum.78
  9.3 0.8 multiply_bitcast_fusion
  10.1 91.0 %all-gather.4.cloned.1.call-done = bf16[512,4096]{0,1:T(8,128)(2,1)} async-done(((bf16[512,64]{0,1:T(8,128)(2,1)}), bf16[512,4096]{0,1:T(8,128)(2,1)}) %all-gather.4.cloned.1.call-update) | async-done | bytes 4194320 | tf_op jit(solution)/shard_map/all_gather | solution.py:78
  101.1 4.6 %convolution_convert_fusion = bf16[128,4096]{1,0:T(8,128)(2,1)} fusion(bf16[512,4096]{0,1:T(8,128)(2,1)} %all-gather.4.cloned.1.call-done, f32[128,512]{1,0:T(8,128)S(1)} %reduce_sum.78), kind=kOutput, calls=%fused_computation.5 | convolution fusion | flops 537526272 | bytes 5505024 | tf_op jit(solution)/shard_map/dot_general | solution.py:76
  106.2 0.3 reshape.203
  106.5 0.6 reduce_sum.77
  107.3 0.7 fusion.38
  108.1 73.3 %all-reduce.2.cloned.1.call-done = bf16[128,4096]{1,0:T(8,128)(2,1)} async-done(((bf16[128,4096]{1,0:T(8,128)(2,1)}), bf16[128,4096]{1,0:T(8,128)(2,1)}) %all-reduce.2.cloned.1.call-update) | async-done | bytes 1048592 | tf_op jit(solution)/shard_map/psum | solution.py:81
  181.4 1.1 convolution_convert_fusion.1
  182.5 0.7 reshape.199
  183.3 14.2 %all-to-all-start = ((bf16[64,2,512]{2,1,0:T(2,128)(2,1)}), bf16[64,2,512]{2,1,0:T(2,128)(2,1)S(1)}, u32[]{:S(2)}, u32[]{:S(2)}) async-start(bf16[64,2,512]{2,1,0:T(2,128)(2,1)} %reshape.199), calls=%async_computation | async-start | bytes 262144 | tf_op jit(solution)/shard_map/all_to_all | solution.py:101
  199.3 0.6 fusion.37
  199.9 1.3 fusion.30
  201.2 6.6 %all-to-all-done = bf16[64,2,512]{2,1,0:T(2,128)(2,1)S(1)} async-done(((bf16[64,2,512]{2,1,0:T(2,128)(2,1)}), bf16[64,2,512]{2,1,0:T(2,128)(2,1)S(1)}, u32[]{:S(2)}, u32[]{:S(2)}) %all-to-all-start) | async-done | bytes 131104 | tf_op jit(solution)/shard_map/all_to_all | solution.py:101
  208.2 1.1 fusion.7
  209.3 0.5 all-gather.8.cloned.1.call-update
  209.9 0.4 fusion.21
  210.3 40.0 %all-gather.6.cloned.1.call-done = bf16[384,4096]{1,0:T(8,128)(2,1)} async-done(((bf16[384,512]{1,0:T(8,128)(2,1)}), bf16[384,4096]{1,0:T(8,128)(2,1)}) %all-gather.6.cloned.1.call-update) | async-done | bytes 3145744 | tf_op jit(solution)/shard_map/all_gather | solution.py:133
  250.3 2.6 fusion
  252.9 85.4 %all-gather.8.cloned.1.call-done = bf16[4096,768]{1,0:T(8,128)(2,1)} async-done(((bf16[64,768]{1,0:T(8,128)(2,1)}), bf16[4096,768]{1,0:T(8,128)(2,1)}) %all-gather.8.cloned.1.call-update) | async-done | bytes 6291472 | tf_op jit(solution)/shard_map/all_gather | solution.py:137
  338.3 6.7 %fusion.3 = f32[384,768]{0,1:T(8,128)S(1)} fusion(bf16[4096,768]{1,0:T(8,128)(2,1)} %all-gather.8.cloned.1.call-done, bf16[384,4096]{1,0:T(8,128)(2,1)} %all-gather.6.cloned.1.call-done, f32[4096]{0:T(1024)S(1)} %copy-done.3, f32[384]{0:T(512)S(1)} %add_rsqrt_fusion), kind=kOutput, calls=%fused_computation.6 | convolution fusion | flops 2422210560 | bytes 10634752 | tf_op jit(solution)/shard_map/dot_general | solution.py:135
  345.2 1.1 copy.18
  (32 shorter events, 1.4 us)
Async XLA Ops:
  6.5 201.7 %copy-start = (bf16[1,256,512]{2,1,0:T(8,128)(2,1)S(1)}, bf16[1,256,512]{2,1,0:T(8,128)(2,1)}, u32[]{:S(2)}) copy-start(bf16[1,256,512]{2,1,0:T(8,128)(2,1)} %param.15) | copy-start | bytes 786436
  6.5 94.5 %all-gather.4.cloned.1.call-start = ((), (), s32[]{:S(2)}) async-start(), calls=%async_computation.1 | async-start | bytes 4259840 | tf_op jit(solution)/shard_map/all_gather | solution.py:78
  7.3 174.2 %all-reduce.2.cloned.1.call-start = ((), (), s32[]{:S(2)}) async-start(), calls=%async_computation.2 | async-start | bytes 2097152 | tf_op jit(solution)/shard_map/psum | solution.py:81
  8.7 97.0 %copy-start.4 = (s32[128]{0:T(128)S(1)}, s32[128]{0:T(128)}, u32[]{:S(2)}) copy-start(s32[128]{0:T(128)} %param.19) | copy-start | bytes 1540
  8.7 97.5 %copy-start.1 = (bf16[512,512]{1,0:T(8,128)(2,1)S(1)}, bf16[512,512]{1,0:T(8,128)(2,1)}, u32[]{:S(2)}) copy-start(bf16[512,512]{1,0:T(8,128)(2,1)} %param.12) | copy-start | bytes 1572868
  10.1 171.3 %copy-start.2 = (f32[512]{0:T(512)S(1)}, f32[512]{0:T(512)}, u32[]{:S(2)}) copy-start(f32[512]{0:T(512)} %param.14) | copy-start | bytes 6148
  106.5 231.8 %copy-start.3 = (f32[4096]{0:T(1024)S(1)}, f32[4096]{0:T(1024)}, u32[]{:S(2)}) copy-start(f32[4096]{0:T(1024)} %param.20) | copy-start | bytes 49156
  183.3 24.5 %all-to-all-start = ((bf16[64,2,512]{2,1,0:T(2,128)(2,1)}), bf16[64,2,512]{2,1,0:T(2,128)(2,1)S(1)}, u32[]{:S(2)}, u32[]{:S(2)}) async-start(bf16[64,2,512]{2,1,0:T(2,128)(2,1)} %reshape.199), calls=%async_computation | async-start | bytes 262144 | tf_op jit(solution)/shard_map/all_to_all | solution.py:101
  197.4 52.9 %all-gather.6.cloned.1.call-start = ((), (), s32[]{:S(2)}) async-start(), calls=%async_computation.3 | async-start | bytes 3538944 | tf_op jit(solution)/shard_map/all_gather | solution.py:133
  209.3 129.0 %all-gather.8.cloned.1.call-start = ((), (), s32[]{:S(2)}) async-start(), calls=%async_computation.4 | async-start | bytes 6389760 | tf_op jit(solution)/shard_map/all_gather | solution.py:137
Sparse Core Ops, SparseCore 0:
  10.7 90.2 all-gather.3
  105.8 75.5 all-reduce.1
  209.4 40.8 all-gather.5
  253.5 84.7 all-gather.7
where the time goes:
time: 353 us
  waiting for transfers between devices  298 us (84%)
  between operations  15.2 us (4%)
  starting transfers between devices  14.3 us (4%)
  matrix products  13.8 us (4%)
  other arithmetic  8.27 us (2%)
  local copies, waits for them, and re-layouts  3.69 us (1%)
    all_gather x1, waiting for transfers between devices, shards(): lax.all_gather(out_weight, 'req', axis=1, tiled=True)  91 us
    all_gather x1, waiting for transfers between devices, shards(): lax.all_gather(qkv_weight, 'req', axis=0, tiled=True)  85.4 us
    psum x1, waiting for transfers between devices, shards(): lax.psum(partial_value.astype(jnp.bfloat16), 'tp').astype(jnp.float32)  73.3 us
    all_gather x1, waiting for transfers between devices, shards(): gathered = lax.all_gather(embedded, 'tp', axis=1, tiled=True)  40 us
    all_to_all x1, starting transfers between devices, shards(): lax.all_to_all(outgoing.reshape(requests, capacity, feature_width), 'req'...  14.2 us
  transfers between devices with their start and end apart: 5, of which 5 were waited for; matrix products, arithmetic and copies ran while one was open for 3% of the time, Pallas kernels for 0%

commit v1 on v0

--- a/solution.py
+++ b/solution.py
@@ -73,10 +73,21 @@
     merged_residual = jnp.mean(
         vision_residual.astype(jnp.float32).reshape(-1, 4, feature_width), axis=1
     )
+
+    def terms_show(raw, chip_axis):
+        tile_out = jnp.concatenate(
+            lax.all_to_all(
+                jnp.stack([raw for _ in range(lax.axis_size(chip_axis))], 0),
+                chip_axis,
+                split_axis=0,
+                concat_axis=0,
+            ),
+            1,
+        )
+        return tile_out
+
     partial_value = jnp.dot(
-        merged_context,
-        lax.all_gather(out_weight, "req", axis=1, tiled=True),
-        preferred_element_type=jnp.float32,
+        merged_context, terms_show(out_weight, chip_axis="req"), preferred_element_type=jnp.float32
     )
     summed = lax.psum(partial_value.astype(jnp.bfloat16), "tp").astype(jnp.float32)
     own_share = lax.dynamic_slice_in_dim(

time: 353 us -> 373 us (1.057)
  starting transfers between devices: 14.3 us -> 26.3 us
  waiting for transfers between devices: 298 us -> 303 us
    all_to_all x0 -> x1, waiting for transfers between devices: none -> 94.9 us  [terms_show(): lax.all_to_all(jnp.stack([raw for _ in range(lax.axis_size(chip_axis))],...]
    all_gather x1 -> x0, waiting for transfers between devices: 91 us -> none  [shards(): lax.all_gather(out_weight, 'req', axis=1, tiled=True)]
    all_to_all x0 -> x1, starting transfers between devices: none -> 12 us  [terms_show(): lax.all_to_all(jnp.stack([raw for _ in range(lax.axis_size(chip_axis))],...]
  transfers between devices with their start and end apart: 5 -> 5, of which waited for: 5 -> 5; matrix products, arithmetic and copies ran while one was open for 3% -> 2% of each run, Pallas kernels for 0% -> 0%
where the time goes in v1:
time: 373 us; the launch traced here: 372 us
  waiting for transfers between devices  303 us (81%)
  starting transfers between devices  26.3 us (7%)
  between operations  15.2 us (4%)
  matrix products  13.8 us (4%)
  other arithmetic  7.52 us (2%)
  local copies, waits for them, and re-layouts  6.01 us (2%)
    all_to_all x1, waiting for transfers between devices, terms_show(): lax.all_to_all(jnp.stack([raw for _ in range(lax.axis_size(chip_axis))],...  94.9 us
    all_gather x1, waiting for transfers between devices, shards(): lax.all_gather(qkv_weight, 'req', axis=0, tiled=True)  85.5 us
    psum x1, waiting for transfers between devices, shards(): lax.psum(partial_value.astype(jnp.bfloat16), 'tp').astype(jnp.float32)  75.8 us
    all_gather x1, waiting for transfers between devices, shards(): gathered = lax.all_gather(embedded, 'tp', axis=1, tiled=True)  39.9 us
    all_to_all x1, starting transfers between devices, shards(): lax.all_to_all(outgoing.reshape(requests, capacity, feature_width), 'req'...  14.2 us
    all_to_all x1, starting transfers between devices, terms_show(): lax.all_to_all(jnp.stack([raw for _ in range(lax.axis_size(chip_axis))],...  12 us
  transfers between devices with their start and end apart: 5, of which 5 were waited for; matrix products, arithmetic and copies ran while one was open for 2% of the time, Pallas kernels for 0%

profile of v1, /device:TPU:1, one launch (start us, length us, event | category | flops | bytes accessed | tf_op | source)
XLA Modules:
  0.0 372.3 jit_solution(16158290020068252007)
XLA Ops:
  6.5 3.4 stack.2
  9.9 12.0 %all-to-all-start = ((bf16[64,512,64]{1,2,0:T(8,128)(2,1)}), bf16[64,512,64]{1,2,0:T(8,128)(2,1)}, u32[]{:S(2)}, u32[]{:S(2)}) async-start(bf16[64,512,64]{1,2,0:T(8,128)(2,1)} %stack.2), calls=%async_computation | async-start | bytes 8388608 | tf_op jit(solution)/shard_map/all_to_all | solution.py:79
  22.0 0.3 reshape.215
  22.4 0.6 reduce_sum.78
  23.0 94.9 %all-to-all-done = bf16[64,512,64]{1,2,0:T(8,128)(2,1)} async-done(((bf16[64,512,64]{1,2,0:T(8,128)(2,1)}), bf16[64,512,64]{1,2,0:T(8,128)(2,1)}, u32[]{:S(2)}, u32[]{:S(2)}) %all-to-all-start) | async-done | bytes 4194336 | tf_op jit(solution)/shard_map/all_to_all | solution.py:79
  117.9 4.7 %convolution_convert_fusion = bf16[128,4096]{1,0:T(8,128)(2,1)} fusion(bf16[512,4096]{0,1:T(8,128)(2,1)} %bitcast.4, f32[128,512]{1,0:T(8,128)S(1)} %reduce_sum.78), kind=kOutput, calls=%fused_computation.5 | convolution fusion | flops 537526272 | bytes 5505024 | tf_op jit(solution)/shard_map/dot_general | solution.py:89
  123.0 0.3 reshape.213
  123.4 0.6 reduce_sum.77
  124.1 0.7 fusion.38
  124.9 75.8 %all-reduce.2.cloned.1.call-done = bf16[128,4096]{1,0:T(8,128)(2,1)} async-done(((bf16[128,4096]{1,0:T(8,128)(2,1)}), bf16[128,4096]{1,0:T(8,128)(2,1)}) %all-reduce.2.cloned.1.call-update) | async-done | bytes 1048592 | tf_op jit(solution)/shard_map/psum | solution.py:92
  200.7 1.1 convolution_convert_fusion.1
  201.8 0.7 reshape.209
  202.5 14.2 %all-to-all-start.1 = ((bf16[64,2,512]{2,1,0:T(2,128)(2,1)}), bf16[64,2,512]{2,1,0:T(2,128)(2,1)S(1)}, u32[]{:S(2)}, u32[]{:S(2)}) async-start(bf16[64,2,512]{2,1,0:T(2,128)(2,1)} %reshape.209), calls=%async_computation.1 | async-start | bytes 262144 | tf_op jit(solution)/shard_map/all_to_all | solution.py:112
  218.6 0.6 fusion.37
  219.2 1.3 fusion.30
  220.4 6.6 %all-to-all-done.1 = bf16[64,2,512]{2,1,0:T(2,128)(2,1)S(1)} async-done(((bf16[64,2,512]{2,1,0:T(2,128)(2,1)}), bf16[64,2,512]{2,1,0:T(2,128)(2,1)S(1)}, u32[]{:S(2)}, u32[]{:S(2)}) %all-to-all-start.1) | async-done | bytes 131104 | tf_op jit(solution)/shard_map/all_to_all | solution.py:112
  227.5 1.1 fusion.7
  228.6 0.7 all-gather.5.cloned.1.call-update
  229.3 0.4 fusion.21
  229.7 39.9 %all-gather.3.cloned.1.call-done = bf16[384,4096]{1,0:T(8,128)(2,1)} async-done(((bf16[384,512]{1,0:T(8,128)(2,1)}), bf16[384,4096]{1,0:T(8,128)(2,1)}) %all-gather.3.cloned.1.call-update) | async-done | bytes 3145744 | tf_op jit(solution)/shard_map/all_gather | solution.py:144
  269.6 2.6 fusion
  272.2 85.5 %all-gather.5.cloned.1.call-done = bf16[4096,768]{1,0:T(8,128)(2,1)} async-done(((bf16[64,768]{1,0:T(8,128)(2,1)}), bf16[4096,768]{1,0:T(8,128)(2,1)}) %all-gather.5.cloned.1.call-update) | async-done | bytes 6291472 | tf_op jit(solution)/shard_map/all_gather | solution.py:148
  357.7 6.7 %fusion.3 = f32[384,768]{0,1:T(8,128)S(1)} fusion(bf16[4096,768]{1,0:T(8,128)(2,1)} %all-gather.5.cloned.1.call-done, bf16[384,4096]{1,0:T(8,128)(2,1)} %all-gather.3.cloned.1.call-done, f32[4096]{0:T(1024)S(1)} %copy-done.4, f32[384]{0:T(512)S(1)} %add_rsqrt_fusion), kind=kOutput, calls=%fused_computation.6 | convolution fusion | flops 2422210560 | bytes 10634752 | tf_op jit(solution)/shard_map/dot_general | solution.py:146
  364.7 1.1 copy.19
  (36 shorter events, 1.4 us)
Async XLA Ops:
  6.5 220.9 %copy-start = (bf16[1,256,512]{2,1,0:T(8,128)(2,1)S(1)}, bf16[1,256,512]{2,1,0:T(8,128)(2,1)}, u32[]{:S(2)}) copy-start(bf16[1,256,512]{2,1,0:T(8,128)(2,1)} %param.15) | copy-start | bytes 786436
  9.9 12.1 %copy-start.1 = (bf16[512,512]{1,0:T(8,128)(2,1)S(1)}, bf16[512,512]{1,0:T(8,128)(2,1)}, u32[]{:S(2)}) copy-start(bf16[512,512]{1,0:T(8,128)(2,1)} %param.11) | copy-start | bytes 1572868
  9.9 13.1 %copy-start.5 = (s32[128,2]{0,1:T(2,128)S(1)}, s32[128,2]{0,1:T(2,128)}, u32[]{:S(2)}) copy-start(s32[128,2]{0,1:T(2,128)} %param.18) | copy-start | bytes 3076
  9.9 108.0 %all-to-all-start = ((bf16[64,512,64]{1,2,0:T(8,128)(2,1)}), bf16[64,512,64]{1,2,0:T(8,128)(2,1)}, u32[]{:S(2)}, u32[]{:S(2)}) async-start(bf16[64,512,64]{1,2,0:T(8,128)(2,1)} %stack.2), calls=%async_computation | async-start | bytes 8388608 | tf_op jit(solution)/shard_map/all_to_all | solution.py:79
  21.9 178.8 %all-reduce.2.cloned.1.call-start = ((), (), s32[]{:S(2)}) async-start(), calls=%async_computation.2 | async-start | bytes 2097152 | tf_op jit(solution)/shard_map/psum | solution.py:92
  22.3 100.2 %copy-start.6 = (s32[128]{0:T(128)S(1)}, s32[128]{0:T(128)}, u32[]{:S(2)}) copy-start(s32[128]{0:T(128)} %param.19) | copy-start | bytes 1540
  22.3 100.7 %copy-start.2 = (bf16[512,512]{1,0:T(8,128)(2,1)S(1)}, bf16[512,512]{1,0:T(8,128)(2,1)}, u32[]{:S(2)}) copy-start(bf16[512,512]{1,0:T(8,128)(2,1)} %param.12) | copy-start | bytes 1572868
  117.9 82.8 %copy-start.3 = (f32[512]{0:T(512)S(1)}, f32[512]{0:T(512)}, u32[]{:S(2)}) copy-start(f32[512]{0:T(512)} %param.14) | copy-start | bytes 6148
  123.3 234.4 %copy-start.4 = (f32[4096]{0:T(1024)S(1)}, f32[4096]{0:T(1024)}, u32[]{:S(2)}) copy-start(f32[4096]{0:T(1024)} %param.20) | copy-start | bytes 49156
  202.5 24.5 %all-to-all-start.1 = ((bf16[64,2,512]{2,1,0:T(2,128)(2,1)}), bf16[64,2,512]{2,1,0:T(2,128)(2,1)S(1)}, u32[]{:S(2)}, u32[]{:S(2)}) async-start(bf16[64,2,512]{2,1,0:T(2,128)(2,1)} %reshape.209), calls=%async_computation.1 | async-start | bytes 262144 | tf_op jit(solution)/shard_map/all_to_all | solution.py:112
  216.7 52.9 %all-gather.3.cloned.1.call-start = ((), (), s32[]{:S(2)}) async-start(), calls=%async_computation.3 | async-start | bytes 3538944 | tf_op jit(solution)/shard_map/all_gather | solution.py:144
  228.6 129.2 %all-gather.5.cloned.1.call-start = ((), (), s32[]{:S(2)}) async-start(), calls=%async_computation.4 | async-start | bytes 6389760 | tf_op jit(solution)/shard_map/all_gather | solution.py:148
Sparse Core Ops, SparseCore 0:
  122.7 77.9 all-reduce.1
  228.7 40.8 all-gather.2
  272.9 84.7 all-gather.4
